TPU v7x, 128 devices: a whole 4x4x4 slice. The times are simulated.
128 devices in a mesh: outer: 4 (over z), inner: 32 (over y, x, core).
Axes of the slice: x: 4, y: 4, z: 4, core: 2. Of those that a mesh axis runs over, the one named last changes fastest.
Arguments:
- tiles: bfloat16 [65536, 128, 128], P(('outer', 'inner')), as said below
- tile_row: int32 [65536], P(('outer', 'inner')), may hold values from 0 to 3, as said below
- tile_col: int32 [65536], P(('outer', 'inner')), may hold values from 0 to 3, as said below
- counts: int32 [16384], P(('outer', 'inner')), may hold values from 1 to 4, as said below
- vectors: bfloat16 [65536, 64], P(('outer', 'inner')), may hold values from -6 to 6
Outputs:
- basis: float32 [65536, 64], P(('outer', 'inner'))
- degree: float32 [65536], P(('outer', 'inner'))
Inputs may be any that keep to these rules, and one draw needn't show every extreme that they name: Slot s from sender g to destination h is live exactly when s < counts[g * 128 + h]; the tiles of dead slots hold values that are no part of P. counts is 4 from every sender to itself and 1 to 4 from every sender to every other destination. `tile_row`: A slot from a sender to itself with number s lies in block row s % 4. `tile_col`: A slot from a sender to itself with number s lies in block column s % 4. `tiles`: entries are affinities, zero or positive.
All inputs are finite; a program needn't handle non-finite values.
Results may differ from a plain program's by a relative error of at most 0.004.
Values may be sent and summed in bfloat16 or wider, within the bound.
No kernel may reach another device: no remote copies, remote signals or barrier semaphores. Data moves between devices by JAX's collectives and lax.ppermute only.
A program may use at most 192 MiB of HBM per device.

v0:
```python
import jax
import jax.numpy as jnp
from jax import lax
from jax.sharding import PartitionSpec as P


def shards(tiles, tile_row, tile_col, counts, vectors):
    peer_count = lax.axis_size(("outer", "inner"))
    slot_count = tiles.shape[0] // peer_count
    tile_size = tiles.shape[1]
    rows_dev = vectors.shape[0]
    block_count = rows_dev // tile_size
    vec_width = vectors.shape[1]
    highest = lax.Precision.HIGHEST
    got_tiles, got_rows, got_cols, got_counts = (
        lax.all_to_all(tiles, ("outer", "inner"), split_axis=0, concat_axis=0, tiled=True),
        lax.all_to_all(tile_row, ("outer", "inner"), split_axis=0, concat_axis=0, tiled=True),
        lax.all_to_all(tile_col, ("outer", "inner"), split_axis=0, concat_axis=0, tiled=True),
        lax.all_to_all(counts, ("outer", "inner"), split_axis=0, concat_axis=0, tiled=True),
    )
    got_sums = jnp.sum(got_tiles, axis=1, dtype=jnp.float32)
    slot_number = jnp.arange(slot_count, dtype=jnp.int32)[None, :]
    own_live = (slot_number < counts[:, None]).reshape(-1).astype(jnp.float32)
    got_live = (slot_number < got_counts[:, None]).reshape(-1).astype(jnp.float32)
    block_ids = jnp.arange(block_count, dtype=jnp.int32)[None, :]
    own_weight = (tile_row[:, None] == block_ids).astype(jnp.float32) * own_live[:, None]
    got_weight = (got_cols[:, None] == block_ids).astype(jnp.float32) * got_live[:, None]
    own_sums = jnp.sum(tiles, axis=2, dtype=jnp.float32)
    degree_blocks = jnp.einsum("tr,ta->ra", own_weight, own_sums, precision=highest)
    degree_blocks = degree_blocks + jnp.einsum("tr,ta->ra", got_weight, got_sums, precision=highest)
    degree = 1.0 + degree_blocks.reshape(rows_dev)
    inv_root = lax.rsqrt(degree)
    scaled = (inv_root[:, None] * vectors.astype(jnp.float32)).astype(jnp.bfloat16)

    def piece_layout(piece, start):
        piece_devs = piece.shape[0] // rows_dev
        first_dev = start // rows_dev
        block_vec = piece.reshape(piece_devs, block_count, tile_size, vec_width)
        source_idx = jnp.repeat(jnp.arange(piece_devs, dtype=jnp.int32), slot_count)
        return (block_vec, source_idx, first_dev * slot_count, piece_devs * slot_count)

    empty = jnp.zeros((block_count, tile_size, vec_width), jnp.float32)
    group_vec = lax.all_gather(scaled, "inner", axis=0, tiled=True)
    piece = lax.all_gather(group_vec, "outer", axis=0, tiled=True)
    start = jnp.int32(0)
    block_vec, source_idx, begin, length = piece_layout(piece, start)
    forward = jnp.einsum(
        "tab,tbk->tak", tiles, block_vec[source_idx, tile_col], preferred_element_type=jnp.float32
    )
    block_vec, source_idx, begin, length = piece_layout(piece, start)
    got_mix = got_weight.astype(jnp.bfloat16)
    mirrored = jnp.einsum(
        "tba,tbk->tak",
        got_tiles,
        block_vec[source_idx, got_rows],
        preferred_element_type=jnp.float32,
    )
    total = jnp.einsum("tr,tak->rak", own_weight, forward, precision=highest) + jnp.einsum(
        "tr,tak->rak", got_mix, mirrored.astype(jnp.bfloat16), preferred_element_type=jnp.float32
    )
    total = total + empty
    image = inv_root[:, None] * (total.reshape(rows_dev, vec_width) + scaled.astype(jnp.float32))
    local_gram = jnp.dot(image.T, image, precision=highest)
    gram = lax.psum(local_gram, ("outer", "inner")) / jnp.float32(rows_dev * peer_count)
    lower = jnp.linalg.cholesky(gram)
    basis = jax.scipy.linalg.solve_triangular(lower, image.T, lower=True).T
    return (basis, degree)


def solution(mesh):
    placed = (
        P(("outer", "inner"), None, None),
        P(("outer", "inner")),
        P(("outer", "inner")),
        P(("outer", "inner")),
        P(("outer", "inner"), None),
    )
    return jax.shard_map(
        shards,
        mesh=mesh,
        in_specs=placed,
        out_specs=(P(("outer", "inner"), None), P(("outer", "inner"))),
        check_vma=False,
    )
```

profile of v0, /device:TPU:1, one launch (start us, length us, event | category | flops | bytes accessed | tf_op | source)
XLA Modules:
  0.0 626.3 jit_solution(13226330766518004586)
XLA Ops:
  7.2 1.4 copy.27
  8.6 11.5 %all-to-all-start.1 = ((s32[128,1,1]{2,1,0:T(1,128)}), s32[128,1,1]{2,1,0:T(1,128)S(1)}, u32[]{:S(2)}, u32[]{:S(2)}) async-start(s32[128,1,1]{2,1,0:T(1,128)} %copy.27), calls=%async_computation.1 | async-start | bytes 131072 | tf_op jit(solution)/shard_map/all_to_all | solution.py:19
  20.9 8.7 %all-to-all-done.1 = s32[128,1,1]{2,1,0:T(1,128)S(1)} async-done(((s32[128,1,1]{2,1,0:T(1,128)}), s32[128,1,1]{2,1,0:T(1,128)S(1)}, u32[]{:S(2)}, u32[]{:S(2)}) %all-to-all-start.1) | async-done | bytes 544 | tf_op jit(solution)/shard_map/all_to_all | solution.py:19
  29.6 13.9 %all_to_all.35 = s32[128,4,1]{1,2,0:T(1,128)S(1)} all-to-all(s32[128,4,1]{1,2,0:T(1,128)S(1)} %bitcast.50), channel_id=1, replica_groups=mesh['outer'=4,'inner'=32] {'outer','inner'}, dimensions={0} | all-to-all | bytes 4096 | tf_op jit(solution)/shard_map/all_to_all | solution.py:18
  43.5 5.6 all-to-all-start.2
  49.4 10.0 %convert_reduce_fusion.1 = f32[512,128]{1,0:T(8,128)S(1)} fusion(bf16[512,128,128]{2,1,0:T(8,128)(2,1)} %param.5), kind=kLoop, calls=%fused_computation.3 | loop fusion | flops 16711680 | bytes 17039360 | tf_op jit(solution)/shard_map/reduce_sum | solution.py:28
  59.7 2.4 reduce.7
  63.5 197.5 %all-to-all-done.2 = bf16[512,128,128]{2,1,0:T(8,128)(2,1)} async-done(((bf16[512,128,128]{2,1,0:T(8,128)(2,1)}), bf16[512,128,128]{2,1,0:T(8,128)(2,1)}, u32[]{:S(2)}, u32[]{:S(2)}) %all-to-all-start.2) | async-done | bytes 16777248 | tf_op jit(solution)/shard_map/all_to_all | solution.py:16
  261.1 6.9 %convert_reduce_fusion = f32[512,128]{1,0:T(8,128)S(1)} fusion(bf16[512,128,128]{2,1,0:T(8,128)(2,1)} %all-to-all-done.2), kind=kLoop, calls=%fused_computation.2 | loop fusion | flops 16711680 | bytes 17039360 | tf_op jit(solution)/shard_map/reduce_sum | solution.py:21
  269.5 75.4 %all-gather.3.cloned.1.call-done = bf16[16384,64]{0,1:T(8,128)(2,1)} async-done(((bf16[512,64]{0,1:T(8,128)(2,1)}), bf16[16384,64]{0,1:T(8,128)(2,1)}) %all-gather.3.cloned.1.call-update) | async-done | bytes 2097168 | tf_op jit(solution)/shard_map/all_gather | solution.py:43
  345.7 7.9 %all-to-all-start.3 = ((s32[128,4,1]{1,2,0:T(1,128)}), s32[128,4,1]{1,2,0:T(1,128)S(1)}, u32[]{:S(2)}, u32[]{:S(2)}) async-start(s32[128,4,1]{1,2,0:T(1,128)} %bitcast.8), calls=%async_computation.3 | async-start | bytes 131072 | tf_op jit(solution)/shard_map/all_to_all | solution.py:17
  353.7 9.4 %all-to-all-done.3 = s32[128,4,1]{1,2,0:T(1,128)S(1)} async-done(((s32[128,4,1]{1,2,0:T(1,128)}), s32[128,4,1]{1,2,0:T(1,128)S(1)}, u32[]{:S(2)}, u32[]{:S(2)}) %all-to-all-start.3) | async-done | bytes 2080 | tf_op jit(solution)/shard_map/all_to_all | solution.py:17
  364.0 65.3 %all-gather.5.cloned.1.call-done = bf16[65536,64]{0,1:T(8,128)(2,1)} async-done(((bf16[16384,64]{0,1:T(8,128)(2,1)}), bf16[65536,64]{0,1:T(8,128)(2,1)}) %all-gather.5.cloned.1.call-update) | async-done | bytes 8388624 | tf_op jit(solution)/shard_map/all_gather | solution.py:44
  429.2 11.8 %reshape.136 = bf16[128,4,128,64]{2,1,0,3:T(4,128)(2,1)} reshape(bf16[65536,64]{0,1:T(8,128)(2,1)} %all-gather.5.cloned.1.call-done) | data formatting | bytes 16777216 | tf_op jit(solution)/shard_map/reshape | solution.py:38
  441.0 16.3 %copy.28 = bf16[128,4,128,64]{2,3,1,0:T(8,128)(2,1)} copy(bf16[128,4,128,64]{2,1,0,3:T(4,128)(2,1)} %reshape.136) | data formatting | bytes 16777216 | tf_op jit(solution)/shard_map/reshape | solution.py:38
  457.3 11.1 %gather_fusion.1 = bf16[512,128,64]{1,2,0:T(8,128)(2,1)} fusion(bf16[128,4,128,64]{2,3,1,0:T(8,128)(2,1)} %copy.28, s32[512]{0:T(512)S(1)} %bitcast.47), kind=kCustom, calls=%fused_computation.1 | custom fusion | bytes 16781312 | tf_op jit(solution)/shard_map/gather | solution.py:55
  468.5 11.0 %gather_fusion = bf16[512,128,64]{1,2,0:T(8,128)(2,1)} fusion(bf16[128,4,128,64]{2,3,1,0:T(8,128)(2,1)} %copy.28, s32[512]{0:T(512)S(1)} %bitcast.46), kind=kCustom, calls=%fused_computation | custom fusion | bytes 16781312 | tf_op jit(solution)/shard_map/gather | solution.py:48
  479.4 19.6 %convolution_bitcast_fusion = f32[512,128,64]{1,2,0:T(8,128)} fusion(bf16[512,128,64]{1,2,0:T(8,128)(2,1)} %gather_fusion, bf16[512,128,128]{2,1,0:T(8,128)(2,1)} %param.5), kind=kOutput, calls=%fused_computation.6 | convolution fusion | flops 1073741824 | bytes 41943040 | tf_op jit(solution)/shard_map/tab,tbk->tak/dot_general | solution.py:47
  499.0 23.4 %fusion = f32[4,128,64]{1,0,2:T(4,128)S(1)} fusion(f32[512,128,64]{1,2,0:T(8,128)} %convolution_bitcast_fusion, f32[512]{0:T(512)S(1)} %reshape.139, s32[512]{0:T(512)S(1)} %copy-done.2), kind=kOutput, calls=%fused_computation.4 | convolution fusion | flops 201330688 | bytes 16912384 | tf_op jit(solution)/shard_map/tr,tak->rak/dot_general | solution.py:58
  522.4 10.5 %convert_bitcast_fusion = bf16[512,128,64]{1,2,0:T(8,128)(2,1)} fusion(bf16[512,128,64]{1,2,0:T(8,128)(2,1)S(1)} %copy-done, bf16[512,128,128]{2,1,0:T(8,128)(2,1)} %all-to-all-done.2), kind=kOutput, calls=%fused_computation.9 | convolution fusion | flops 1077936128 | bytes 33554432 | tf_op jit(solution)/shard_map/tba,tbk->tak/dot_general | solution.py:52
  532.9 7.9 %fusion.4 = f32[4,128,64]{1,0,2:T(4,128)S(1)} fusion(f32[4,128,64]{1,0,2:T(4,128)S(1)} %fusion, bf16[512,128,64]{1,2,0:T(8,128)(2,1)} %convert_bitcast_fusion, f32[512]{0:T(512)S(1)} %reshape.140, s32[512]{0:T(512)S(1)} %eq.31), kind=kOutput, calls=%fused_computation.10 | convolution fusion | flops 33591296 | bytes 8654848 | tf_op jit(solution)/shard_map/tr,tak->rak/dot_general | solution.py:58
  541.1 65.0 %psum.7 = f32[64,64]{0,1:T(8,128)S(1)} all-reduce(f32[64,64]{0,1:T(8,128)S(1)} %fusion.12), channel_id=1, replica_groups=mesh['outer'=4,'inner'=32] {'outer','inner'}, use_global_device_ids=true, to_apply=%region_2.0 | all-reduce | flops 4096 | bytes 32768 | tf_op jit(solution)/shard_map/psum | solution.py:64
  606.2 5.8 cholesky.16
  613.3 4.9 custom-call.7
  (40 shorter events, 8.7 us)
Async XLA Ops:
  8.6 21.0 %all-to-all-start.1 = ((s32[128,1,1]{2,1,0:T(1,128)}), s32[128,1,1]{2,1,0:T(1,128)S(1)}, u32[]{:S(2)}, u32[]{:S(2)}) async-start(s32[128,1,1]{2,1,0:T(1,128)} %copy.27), calls=%async_computation.1 | async-start | bytes 131072 | tf_op jit(solution)/shard_map/all_to_all | solution.py:19
  43.5 5.7 copy-start.4
  43.5 217.6 %all-to-all-start.2 = ((bf16[512,128,128]{2,1,0:T(8,128)(2,1)}), bf16[512,128,128]{2,1,0:T(8,128)(2,1)}, u32[]{:S(2)}, u32[]{:S(2)}) async-start(bf16[512,128,128]{2,1,0:T(8,128)(2,1)} %param.5), calls=%async_computation.2 | async-start | bytes 33554432 | tf_op jit(solution)/shard_map/all_to_all | solution.py:16
  49.1 10.3 %copy-start.2 = (s32[512]{0:T(512)S(1)}, s32[512]{0:T(512)}, u32[]{:S(2)}) copy-start(s32[512]{0:T(512)} %param.6) | copy-start | bytes 6148
  49.1 295.8 %all-gather.3.cloned.1.call-start = ((), (), s32[]{:S(2)}) async-start(), calls=%async_computation.4 | async-start | bytes 2162688 | tf_op jit(solution)/shard_map/all_gather | solution.py:43
  49.4 219.4 %copy-start.1 = (bf16[512,64]{0,1:T(8,128)(2,1)S(1)}, bf16[512,64]{0,1:T(8,128)(2,1)}, u32[]{:S(2)}) copy-start(bf16[512,64]{0,1:T(8,128)(2,1)} %param.9) | copy-start | bytes 196612
  49.4 304.2 %copy-start.3 = (s32[512]{0:T(512)S(1)}, s32[512]{0:T(512)}, u32[]{:S(2)}) copy-start(s32[512]{0:T(512)} %param.7) | copy-start | bytes 6148
  269.5 159.8 %all-gather.5.cloned.1.call-start = ((), (), s32[]{:S(2)}) async-start(), calls=%async_computation.5 | async-start | bytes 10485760 | tf_op jit(solution)/shard_map/all_gather | solution.py:44
  345.7 17.5 %all-to-all-start.3 = ((s32[128,4,1]{1,2,0:T(1,128)}), s32[128,4,1]{1,2,0:T(1,128)S(1)}, u32[]{:S(2)}, u32[]{:S(2)}) async-start(s32[128,4,1]{1,2,0:T(1,128)} %bitcast.8), calls=%async_computation.3 | async-start | bytes 131072 | tf_op jit(solution)/shard_map/all_to_all | solution.py:17
  499.0 23.4 %copy-start = (bf16[512,128,64]{1,2,0:T(8,128)(2,1)S(1)}, bf16[512,128,64]{1,2,0:T(8,128)(2,1)}, u32[]{:S(2)}) copy-start(bf16[512,128,64]{1,2,0:T(8,128)(2,1)} %gather_fusion.1) | copy-start | bytes 25165828
Sparse Core Ops, SparseCore 0:
  269.6 75.2 all-gather.2
  346.6 82.6 all-gather.4
where the time goes:
time: 632 us; the launch traced here: 626 us
  waiting for transfers between devices  356 us (56%)
  blocking collectives  78.9 us (12%)
  matrix products  63.7 us (10%)
  local copies, waits for them, and re-layouts  54.2 us (9%)
  other arithmetic  33.5 us (5%)
  starting transfers between devices  25.1 us (4%)
  between operations  14.5 us (2%)
    all_to_all x1, waiting for transfers between devices, shards(): lax.all_to_all(tiles, ('outer', 'inner'), split_axis=0, concat_axis=0, ti...  198 us
    all_gather x1, waiting for transfers between devices, shards(): group_vec = lax.all_gather(scaled, 'inner', axis=0, tiled=True)  75.4 us
    all_gather x1, waiting for transfers between devices, shards(): piece = lax.all_gather(group_vec, 'outer', axis=0, tiled=True)  65.3 us
    psum x1, blocking collectives, shards(): lax.psum(local_gram, ('outer', 'inner'))  65 us
    reshape x2, local copies, waits for them, and re-layouts, piece_layout(): block_vec = piece.reshape(piece_devs, block_count, tile_size, vec_width)  28.1 us
    dot_general x1, matrix products, shards(): jnp.einsum('tr,tak->rak', own_weight, forward, precision=highest)  23.4 us
    dot_general x1, matrix products, shards(): jnp.einsum('tab,tbk->tak', tiles, block_vec[source_idx, tile_col], prefer...  19.6 us
    all_to_all x1, blocking collectives, shards(): lax.all_to_all(tile_col, ('outer', 'inner'), split_axis=0, concat_axis=0,...  13.9 us
  transfers between devices with their start and end apart: 5, of which 5 were waited for; matrix products, arithmetic and copies ran while one was open for 2% of the time, Pallas kernels for 0%

commit v1 on v0

--- a/solution.py
+++ b/solution.py
@@ -2,6 +2,28 @@
 import jax.numpy as jnp
 from jax import lax
 from jax.sharding import PartitionSpec as P
+
+
+def in_order(blocks, dim):
+    dims = list(blocks.shape[1:])
+    dims[dim] *= blocks.shape[0]
+    return jnp.moveaxis(blocks, 0, dim).reshape(dims)
+
+
+def gather_around(x, axis, dim):
+    size = lax.axis_size(axis)
+    pairs = [(i, (i + 1) % size) for i in range(size)]
+    back = [(b, a) for a, b in pairs]
+    lower, upper = ([], [])
+    for turn in range(size - 1):
+        if turn % 2 == 0:
+            lower.append(lax.ppermute(lower[-1] if lower else x, axis, pairs))
+        else:
+            upper.append(lax.ppermute(upper[-1] if upper else x, axis, back))
+    blocks = jnp.stack([*lower[::-1], x, *upper])
+    shift = lax.axis_index(axis) - len(lower)
+    blocks = blocks[(jnp.arange(size) - shift) % size]
+    return in_order(blocks, dim)
 
 
 def shards(tiles, tile_row, tile_col, counts, vectors):
@@ -41,7 +63,7 @@
 
     empty = jnp.zeros((block_count, tile_size, vec_width), jnp.float32)
     group_vec = lax.all_gather(scaled, "inner", axis=0, tiled=True)
-    piece = lax.all_gather(group_vec, "outer", axis=0, tiled=True)
+    piece = gather_around(group_vec, "outer", 0)
     start = jnp.int32(0)
     block_vec, source_idx, begin, length = piece_layout(piece, start)
     forward = jnp.einsum(

time: 632 us -> 691 us (1.093)
  local copies, waits for them, and re-layouts: 54.2 us -> 83.9 us
  waiting for transfers between devices: 356 us -> 368 us
  other arithmetic: 33.5 us -> 45.2 us
    all_gather x1 -> x0, waiting for transfers between devices: 65.3 us -> none  [shards(): piece = lax.all_gather(group_vec, 'outer', axis=0, tiled=True)]
    ppermute x0 -> x3, waiting for transfers between devices: none -> 45.7 us  [the longest x2 45.7 us: gather_around(): lower.append(lax.ppermute(lower[-1] if lower else x, axis, pairs))]
    another operation x0 -> x2, local copies, waits for them, and re-layouts: none -> 32.2 us  [piece_layout(): block_vec = piece.reshape(piece_devs, block_count, tile_size, vec_width)]
    all_to_all x1, waiting for transfers between devices: 9.39 us -> 40.5 us  [shards(): lax.all_to_all(tile_row, ('outer', 'inner'), split_axis=0, concat_axis=0,...]
    reshape x2 -> x0, local copies, waits for them, and re-layouts: 28.1 us -> none  [piece_layout(): block_vec = piece.reshape(piece_devs, block_count, tile_size, vec_width)]
    gather x0 -> x3, local copies, waits for them, and re-layouts: none -> 13.6 us  [gather_around(): blocks = blocks[(jnp.arange(size) - shift) % size]]
    unnamed x10 -> x11, local copies, waits for them, and re-layouts: 0.03 us -> 12.1 us
    unnamed x0 -> x1, other arithmetic: none -> 7.56 us
  transfers between devices with their start and end apart: 5 -> 7, of which waited for: 5 -> 5; matrix products, arithmetic and copies ran while one was open for 2% -> 2% of each run, Pallas kernels for 0% -> 0%
where the time goes in v1:
time: 691 us; the launch traced here: 681 us
  waiting for transfers between devices  368 us (53%)
  local copies, waits for them, and re-layouts  83.9 us (12%)
  blocking collectives  77.8 us (11%)
  matrix products  63.9 us (9%)
  other arithmetic  45.2 us (7%)
  starting transfers between devices  28.1 us (4%)
  between operations  14.7 us (2%)
    all_to_all x1, waiting for transfers between devices, shards(): lax.all_to_all(tiles, ('outer', 'inner'), split_axis=0, concat_axis=0, ti...  197 us
    all_gather x1, waiting for transfers between devices, shards(): group_vec = lax.all_gather(scaled, 'inner', axis=0, tiled=True)  75.4 us
    psum x1, blocking collectives, shards(): lax.psum(local_gram, ('outer', 'inner'))  63.9 us
    ppermute x2, waiting for transfers between devices, gather_around(): lower.append(lax.ppermute(lower[-1] if lower else x, axis, pairs))  45.7 us
    all_to_all x1, waiting for transfers between devices, shards(): lax.all_to_all(tile_row, ('outer', 'inner'), split_axis=0, concat_axis=0,...  40.5 us
    another operation x2, local copies, waits for them, and re-layouts, piece_layout(): block_vec = piece.reshape(piece_devs, block_count, tile_size, vec_width)  32.2 us
    dot_general x1, matrix products, shards(): jnp.einsum('tr,tak->rak', own_weight, forward, precision=highest)  23.4 us
    dot_general x1, matrix products, shards(): jnp.einsum('tab,tbk->tak', tiles, block_vec[source_idx, tile_col], prefer...  19.8 us
  transfers between devices with their start and end apart: 7, of which 5 were waited for; matrix products, arithmetic and copies ran while one was open for 2% of the time, Pallas kernels for 0%

profile of v1, /device:TPU:1, one launch (start us, length us, event | category | flops | bytes accessed | tf_op | source)
XLA Modules:
  0.0 681.3 jit_solution(9434936243840432665)
XLA Ops:
  8.6 11.5 %all-to-all-start.1 = ((s32[128,1,1]{2,1,0:T(1,128)}), s32[128,1,1]{2,1,0:T(1,128)S(1)}, u32[]{:S(2)}, u32[]{:S(2)}) async-start(s32[128,1,1]{2,1,0:T(1,128)} %copy.30), calls=%async_computation.1 | async-start | bytes 131072 | tf_op jit(solution)/shard_map/all_to_all | solution.py:41
  20.9 8.7 %all-to-all-done.1 = s32[128,1,1]{2,1,0:T(1,128)S(1)} async-done(((s32[128,1,1]{2,1,0:T(1,128)}), s32[128,1,1]{2,1,0:T(1,128)S(1)}, u32[]{:S(2)}, u32[]{:S(2)}) %all-to-all-start.1) | async-done | bytes 544 | tf_op jit(solution)/shard_map/all_to_all | solution.py:41
  29.6 13.9 %all_to_all.35 = s32[128,4,1]{1,2,0:T(1,128)S(1)} all-to-all(s32[128,4,1]{1,2,0:T(1,128)S(1)} %bitcast.58), channel_id=1, replica_groups=mesh['outer'=4,'inner'=32] {'outer','inner'}, dimensions={0} | all-to-all | bytes 4096 | tf_op jit(solution)/shard_map/all_to_all | solution.py:40
  43.5 5.6 all-to-all-start.2
  49.4 10.0 %convert_reduce_fusion.1 = f32[512,128]{1,0:T(8,128)S(1)} fusion(bf16[512,128,128]{2,1,0:T(8,128)(2,1)} %param.5), kind=kLoop, calls=%fused_computation.5 | loop fusion | flops 16711680 | bytes 17039360 | tf_op jit(solution)/shard_map/reduce_sum | solution.py:50
  63.7 197.4 %all-to-all-done.2 = bf16[512,128,128]{2,1,0:T(8,128)(2,1)} async-done(((bf16[512,128,128]{2,1,0:T(8,128)(2,1)}), bf16[512,128,128]{2,1,0:T(8,128)(2,1)}, u32[]{:S(2)}, u32[]{:S(2)}) %all-to-all-start.2) | async-done | bytes 16777248 | tf_op jit(solution)/shard_map/all_to_all | solution.py:38
  261.1 6.9 %convert_reduce_fusion = f32[512,128]{1,0:T(8,128)S(1)} fusion(bf16[512,128,128]{2,1,0:T(8,128)(2,1)} %all-to-all-done.2), kind=kLoop, calls=%fused_computation.4 | loop fusion | flops 16711680 | bytes 17039360 | tf_op jit(solution)/shard_map/reduce_sum | solution.py:43
  269.5 75.4 %all-gather.2.cloned.1.call-done = bf16[16384,64]{0,1:T(8,128)(2,1)} async-done(((bf16[512,64]{0,1:T(8,128)(2,1)}), bf16[16384,64]{0,1:T(8,128)(2,1)}) %all-gather.2.cloned.1.call-update) | async-done | bytes 2097168 | tf_op jit(solution)/shard_map/all_gather | solution.py:65
  347.6 45.7 %collective-permute-done = bf16[16384,64]{0,1:T(8,128)(2,1)S(1)} collective-permute-done((bf16[16384,64]{0,1:T(8,128)(2,1)}, bf16[16384,64]{0,1:T(8,128)(2,1)S(1)}, u32[]{:S(2)}, u32[]{:S(2)}) %collective-permute-start) | collective-permute-done | bytes 2097184 | tf_op jit(solution)/shard_map/ppermute | solution.py:20
  394.2 8.1 %all-to-all-start.3 = ((s32[128,4,1]{1,2,0:T(1,128)}), s32[128,4,1]{1,2,0:T(1,128)S(1)}, u32[]{:S(2)}, u32[]{:S(2)}) async-start(s32[128,4,1]{1,2,0:T(1,128)} %bitcast.13), calls=%async_computation.3 | async-start | bytes 131072 | tf_op jit(solution)/shard_map/all_to_all | solution.py:39
  402.5 40.5 %all-to-all-done.3 = s32[128,4,1]{1,2,0:T(1,128)S(1)} async-done(((s32[128,4,1]{1,2,0:T(1,128)}), s32[128,4,1]{1,2,0:T(1,128)S(1)}, u32[]{:S(2)}, u32[]{:S(2)}) %all-to-all-start.3) | async-done | bytes 2080 | tf_op jit(solution)/shard_map/all_to_all | solution.py:39
  451.4 5.0 gather_fusion.2
  461.3 7.6 %pad_maximum_fusion.1 = bf16[4,16384,64]{1,2,0:T(8,128)(2,1)} fusion(bf16[4,8192,64]{1,2,0:T(8,128)(2,1)} %gather_fusion.3, bf16[4,8192,64]{1,2,0:T(8,128)(2,1)} %gather_fusion.2), kind=kLoop, calls=%fused_computation.10 | loop fusion | flops 16777216 | bytes 16777216
  468.9 12.1 %copy.31 = bf16[4,16384,64]{1,0,2:T(4,128)(2,1)} copy(bf16[4,16384,64]{1,2,0:T(8,128)(2,1)} %pad_maximum_fusion.1) | data formatting | bytes 16777216
  481.0 15.9 %reshape_reshape.4 = bf16[128,4,128,64]{2,1,0,3:T(4,128)(2,1)} reshape(bf16[4,16384,64]{1,0,2:T(4,128)(2,1)} %copy.31) | data formatting | bytes 16777216 | tf_op jit(solution)/shard_map/reshape;reshape | solution.py:60
  496.8 16.3 %copy.32 = bf16[128,4,128,64]{2,3,1,0:T(8,128)(2,1)} copy(bf16[128,4,128,64]{2,1,0,3:T(4,128)(2,1)} %reshape_reshape.4) | data formatting | bytes 16777216 | tf_op jit(solution)/shard_map/reshape;reshape | solution.py:60
  513.2 11.0 %gather_fusion.1 = bf16[512,128,64]{1,2,0:T(8,128)(2,1)} fusion(bf16[128,4,128,64]{2,3,1,0:T(8,128)(2,1)} %copy.32, s32[512]{0:T(512)S(1)} %bitcast.53), kind=kCustom, calls=%fused_computation.1 | custom fusion | bytes 16781312 | tf_op jit(solution)/shard_map/gather | solution.py:77
  524.1 11.0 %gather_fusion = bf16[512,128,64]{1,2,0:T(8,128)(2,1)} fusion(bf16[128,4,128,64]{2,3,1,0:T(8,128)(2,1)} %copy.32, s32[512]{0:T(512)S(1)} %bitcast.52), kind=kCustom, calls=%fused_computation | custom fusion | bytes 16781312 | tf_op jit(solution)/shard_map/gather | solution.py:70
  535.1 19.8 %convolution_bitcast_fusion = f32[512,128,64]{1,2,0:T(8,128)} fusion(bf16[512,128,64]{1,2,0:T(8,128)(2,1)} %gather_fusion, bf16[512,128,128]{2,1,0:T(8,128)(2,1)} %param.5), kind=kOutput, calls=%fused_computation.8 | convolution fusion | flops 1073741824 | bytes 41943040 | tf_op jit(solution)/shard_map/tab,tbk->tak/dot_general | solution.py:69
  554.9 23.4 %fusion = f32[4,128,64]{1,0,2:T(4,128)S(1)} fusion(f32[512,128,64]{1,2,0:T(8,128)} %convolution_bitcast_fusion, f32[512]{0:T(512)S(1)} %reshape.183, s32[512]{0:T(512)S(1)} %copy-done.2), kind=kOutput, calls=%fused_computation.6 | convolution fusion | flops 201330688 | bytes 16912384 | tf_op jit(solution)/shard_map/tr,tak->rak/dot_general | solution.py:80
  578.2 10.6 %convert_bitcast_fusion = bf16[512,128,64]{1,2,0:T(8,128)(2,1)} fusion(bf16[512,128,64]{1,2,0:T(8,128)(2,1)S(1)} %copy-done, bf16[512,128,128]{2,1,0:T(8,128)(2,1)} %all-to-all-done.2), kind=kOutput, calls=%fused_computation.13 | convolution fusion | flops 1077936128 | bytes 33554432 | tf_op jit(solution)/shard_map/tba,tbk->tak/dot_general | solution.py:74
  588.8 7.9 %fusion.4 = f32[4,128,64]{1,0,2:T(4,128)S(1)} fusion(f32[4,128,64]{1,0,2:T(4,128)S(1)} %fusion, bf16[512,128,64]{1,2,0:T(8,128)(2,1)} %convert_bitcast_fusion, f32[512]{0:T(512)S(1)} %reshape.184, s32[512]{0:T(512)S(1)} %eq.33), kind=kOutput, calls=%fused_computation.14 | convolution fusion | flops 33591296 | bytes 8654848 | tf_op jit(solution)/shard_map/tr,tak->rak/dot_general | solution.py:80
  596.9 63.9 %psum.7 = f32[64,64]{0,1:T(8,128)S(1)} all-reduce(f32[64,64]{0,1:T(8,128)S(1)} %fusion.12), channel_id=1, replica_groups=mesh['outer'=4,'inner'=32] {'outer','inner'}, use_global_device_ids=true, to_apply=%region_2.3 | all-reduce | flops 4096 | bytes 32768 | tf_op jit(solution)/shard_map/psum | solution.py:86
  660.9 5.8 cholesky.16
  (51 shorter events, 32.8 us)
Async XLA Ops:
  8.6 21.0 %all-to-all-start.1 = ((s32[128,1,1]{2,1,0:T(1,128)}), s32[128,1,1]{2,1,0:T(1,128)S(1)}, u32[]{:S(2)}, u32[]{:S(2)}) async-start(s32[128,1,1]{2,1,0:T(1,128)} %copy.30), calls=%async_computation.1 | async-start | bytes 131072 | tf_op jit(solution)/shard_map/all_to_all | solution.py:41
  43.5 5.7 copy-start.4
  43.5 217.6 %all-to-all-start.2 = ((bf16[512,128,128]{2,1,0:T(8,128)(2,1)}), bf16[512,128,128]{2,1,0:T(8,128)(2,1)}, u32[]{:S(2)}, u32[]{:S(2)}) async-start(bf16[512,128,128]{2,1,0:T(8,128)(2,1)} %param.5), calls=%async_computation.2 | async-start | bytes 33554432 | tf_op jit(solution)/shard_map/all_to_all | solution.py:38
  49.1 295.8 %all-gather.2.cloned.1.call-start = ((), (), s32[]{:S(2)}) async-start(), calls=%async_computation.4 | async-start | bytes 2162688 | tf_op jit(solution)/shard_map/all_gather | solution.py:65
  49.4 10.0 %copy-start.2 = (s32[512]{0:T(512)S(1)}, s32[512]{0:T(512)}, u32[]{:S(2)}) copy-start(s32[512]{0:T(512)} %param.6) | copy-start | bytes 6148
  63.7 205.1 %copy-start.1 = (bf16[512,64]{0,1:T(8,128)(2,1)S(1)}, bf16[512,64]{0,1:T(8,128)(2,1)}, u32[]{:S(2)}) copy-start(bf16[512,64]{0,1:T(8,128)(2,1)} %param.9) | copy-start | bytes 196612
  63.7 338.6 %copy-start.3 = (s32[512]{0:T(512)S(1)}, s32[512]{0:T(512)}, u32[]{:S(2)}) copy-start(s32[512]{0:T(512)} %param.7) | copy-start | bytes 6148
  344.9 48.4 %collective-permute-start = (bf16[16384,64]{0,1:T(8,128)(2,1)}, bf16[16384,64]{0,1:T(8,128)(2,1)S(1)}, u32[]{:S(2)}, u32[]{:S(2)}) collective-permute-start(bf16[16384,64]{0,1:T(8,128)(2,1)} %all-gather.2.cloned.1.call-done), channel_id=1, source_target_pairs={{0,32},{32,64},{64,96},{96,0},{1,33},{33,65},{65,97},{97,1},{2,34}... | collective-permute-start | bytes 6291464 | tf_op jit(solution)/shard_map/ppermute | solution.py:20
  346.2 97.7 %collective-permute-start.2 = (bf16[16384,64]{0,1:T(8,128)(2,1)}, bf16[16384,64]{0,1:T(8,128)(2,1)}, u32[]{:S(2)}, u32[]{:S(2)}) collective-permute-start(bf16[16384,64]{0,1:T(8,128)(2,1)} %all-gather.2.cloned.1.call-done), channel_id=1, source_target_pairs={{32,0},{64,32},{96,64},{0,96},{33,1},{65,33},{97,65},{1,97},{34,2}... | collective-permute-start | bytes 6291464 | tf_op jit(solution)/shard_map/ppermute | solution.py:22
  393.3 50.6 %collective-permute-start.1 = (bf16[16384,64]{0,1:T(8,128)(2,1)S(1)}, bf16[16384,64]{0,1:T(8,128)(2,1)}, u32[]{:S(2)}, u32[]{:S(2)}) collective-permute-start(bf16[16384,64]{0,1:T(8,128)(2,1)S(1)} %collective-permute-done), channel_id=1, source_target_pairs={{0,32},{32,64},{64,96},{96,0},{1,33},{33,65},{65,97},{97,1},{2,34}... | collective-permute-start | bytes 6291464 | tf_op jit(solution)/shard_map/ppermute | solution.py:20
  394.2 48.7 %all-to-all-start.3 = ((s32[128,4,1]{1,2,0:T(1,128)}), s32[128,4,1]{1,2,0:T(1,128)S(1)}, u32[]{:S(2)}, u32[]{:S(2)}) async-start(s32[128,4,1]{1,2,0:T(1,128)} %bitcast.13), calls=%async_computation.3 | async-start | bytes 131072 | tf_op jit(solution)/shard_map/all_to_all | solution.py:39
  554.9 23.4 %copy-start = (bf16[512,128,64]{1,2,0:T(8,128)(2,1)S(1)}, bf16[512,128,64]{1,2,0:T(8,128)(2,1)}, u32[]{:S(2)}) copy-start(bf16[512,128,64]{1,2,0:T(8,128)(2,1)} %gather_fusion.1) | copy-start | bytes 25165828
Sparse Core Ops, SparseCore 0:
  269.6 75.2 all-gather.1
